TPU v7x, 256 devices: a whole 4x4x8 slice. The times are simulated.
256 devices in a mesh: dp: 32 (over z, y), expert: 8 (over x, core).
Axes of the slice: x: 4, y: 4, z: 8, core: 2. Of those that a mesh axis runs over, the one named last changes fastest.
Arguments:
- residual: bfloat16 [2048, 4096], P(('dp', 'expert')), may hold values from -8.2 to 8.2
- queries: bfloat16 [2048, 4096], P('dp', 'expert'), may hold values from -24 to 24
- new_keys: bfloat16 [2048, 1024], P('dp', 'expert'), may hold values from -6 to 6
- new_values: bfloat16 [2048, 1024], P('dp', 'expert'), may hold values from -6 to 6
- cache_keys: bfloat16 [64, 1024, 1024], P('dp', None, 'expert'), may hold values from -8 to 8
- cache_values: bfloat16 [64, 1024, 1024], P('dp', None, 'expert'), may hold values from -6 to 6
- out_weight: bfloat16 [4096, 4096], P('expert', 'dp'), may hold values from -1 to 1
- ffn_gain: float32 [4096], replicated, may hold values from 0.1 to 1.9
- router: bfloat16 [4096, 8], replicated, may hold values from -0.0234375 to 0.0234375
- routes: int32 [2048, 2], P(('dp', 'expert')), may hold values from 0 to 7, all different within a row; in each aligned block of 64 rows (0 to 63, 64 to 127, ...) at most 24 rows name the same one
- w_gate: bfloat16 [8, 4096, 14336], P('expert', None, 'dp'), may hold values from -0.09375 to 0.09375
- w_up: bfloat16 [8, 4096, 14336], P('expert', None, 'dp'), may hold values from -0.09375 to 0.09375
- w_down: bfloat16 [8, 14336, 4096], P('expert', 'dp'), may hold values from -0.046875 to 0.046875
- summary_gain: float32 [4096], P('expert'), may hold values from 0.1 to 1.9
- reduce_scale: float32 [32], P('expert'), may hold values from 0.1 to 30
- assign: int32 [64], replicated, may hold values from 0 to 3
Outputs:
- summary: bfloat16 [64, 4096], P('dp', 'expert')
- reduced: bfloat16 [64, 4096], P('dp', 'expert')
Inputs may be any that keep to these rules, and one draw needn't show every extreme that they name: `routes`: each token names 2 different experts and every expert is named by some token; among the tokens of one dp index (aligned blocks of 64 rows) no expert is named by more than 24 tokens, and that bound is reached in some block.
All inputs are finite; a program needn't handle non-finite values.
Results may differ from a plain program's by a relative error of at most 0.017.
Values may be sent and summed in bfloat16 or wider, within the bound.
No kernel may reach another device: no remote copies, remote signals or barrier semaphores. Data moves between devices by JAX's collectives and lax.ppermute only.
A program may use at most 128 MiB of HBM per device.

v0:
```python
import math
import jax
import jax.numpy as jnp
from jax import lax
from jax.sharding import PartitionSpec as P

HEADS = 32
KVH = 8
HD = 128
EXPERTS = 8
WIN = 32
GROUP_CAP = 24
EPSILON = 1e-05


def attend(queries, new_keys, new_values, cache_keys, cache_values):
    span_count, cache_len, kv_width = cache_keys.shape
    kv_local = kv_width // HD
    group = HEADS // KVH
    window = queries.shape[0] // span_count
    query_view = queries.reshape(span_count, window, kv_local, group, HD)
    fresh_keys = new_keys.reshape(span_count, window, kv_local, HD)
    fresh_values = new_values.reshape(span_count, window, kv_local, HD)
    stored_keys = cache_keys.reshape(span_count, cache_len, kv_local, HD)
    stored_values = cache_values.reshape(span_count, cache_len, kv_local, HD)
    factor = 1.0 / math.sqrt(HD)
    past_scores = (
        jnp.einsum("ctkgd,cpkd->ckgtp", query_view, stored_keys, preferred_element_type=jnp.float32)
        * factor
    )
    fresh_scores = (
        jnp.einsum("ctkgd,cskd->ckgts", query_view, fresh_keys, preferred_element_type=jnp.float32)
        * factor
    )
    causal = jnp.arange(window)[:, None] >= jnp.arange(window)[None, :]
    fresh_scores = jnp.where(causal, fresh_scores, -jnp.inf)
    highest = jnp.maximum(jnp.max(past_scores, axis=-1), jnp.max(fresh_scores, axis=-1))[..., None]
    past_exp = jnp.exp(past_scores - highest)
    fresh_exp = jnp.exp(fresh_scores - highest)
    totals = jnp.sum(past_exp, axis=-1, keepdims=True) + jnp.sum(fresh_exp, axis=-1, keepdims=True)
    past_weights = (past_exp / totals).astype(jnp.bfloat16)
    fresh_weights = (fresh_exp / totals).astype(jnp.bfloat16)
    context = jnp.einsum(
        "ckgtp,cpkd->ctkgd", past_weights, stored_values, preferred_element_type=jnp.float32
    )
    context = context + jnp.einsum(
        "ckgts,cskd->ctkgd", fresh_weights, fresh_values, preferred_element_type=jnp.float32
    )
    return context.astype(jnp.bfloat16).reshape(span_count * window, kv_local * group * HD)


def expert_rows(rows, w_gate, w_up, w_down):
    gate_proj = jnp.einsum("ned,edf->nef", rows, w_gate, preferred_element_type=jnp.float32)
    up_proj = jnp.einsum("ned,edf->nef", rows, w_up, preferred_element_type=jnp.float32)
    hidden = (jax.nn.silu(gate_proj) * up_proj).astype(jnp.bfloat16)
    return jnp.einsum("nef,efd->ned", hidden, w_down, preferred_element_type=jnp.float32)


def shards(
    residual,
    queries,
    new_keys,
    new_values,
    cache_keys,
    cache_values,
    out_weight,
    ffn_gain,
    router,
    routes,
    w_gate,
    w_up,
    w_down,
    summary_gain,
    reduce_scale,
    assign,
):
    expert_count = lax.axis_size("expert")
    dp_index = lax.axis_index("dp")
    column = lax.axis_index("expert")
    span_local = cache_keys.shape[0]
    tok_local = residual.shape[0]
    width = residual.shape[1]
    slice_width = width // expert_count
    highest_precision = lax.Precision.HIGHEST
    attended = attend(queries, new_keys, new_values, cache_keys, cache_values)
    head_terms = jnp.dot(
        attended,
        lax.all_gather(out_weight, "dp", axis=1, tiled=True),
        preferred_element_type=jnp.float32,
    )
    mixed = residual.astype(jnp.float32) + lax.psum_scatter(
        head_terms, "expert", scatter_dimension=0, tiled=True
    )
    normed = (
        mixed * lax.rsqrt(jnp.mean(mixed * mixed, axis=-1, keepdims=True) + EPSILON) * ffn_gain
    ).astype(jnp.bfloat16)
    logits = jnp.dot(normed, router, preferred_element_type=jnp.float32)
    expert_ids = jnp.arange(EXPERTS, dtype=jnp.int32)
    first = routes[:, 0:1] == expert_ids[None, :]
    second = routes[:, 1:2] == expert_ids[None, :]
    first_logit = jnp.sum(jnp.where(first, logits, 0.0), axis=-1)
    second_logit = jnp.sum(jnp.where(second, logits, 0.0), axis=-1)
    partner = jnp.where(first, routes[:, 1:2], jnp.where(second, routes[:, 0:1], -1))
    outgoing = jnp.where((partner >= 0).T[:, :, None], normed[None, :, :], 0)
    arrived_rows, arrived_partner = (
        lax.all_to_all(outgoing, "expert", split_axis=0, concat_axis=1, tiled=True),
        lax.all_to_all(partner.T, "expert", split_axis=0, concat_axis=1, tiled=True),
    )
    present = (arrived_partner >= 0).astype(jnp.int32)
    position = jnp.cumsum(present, axis=1) - 1
    picker = (present[:, None, :] > 0) & (
        position[:, None, :] == jnp.arange(GROUP_CAP)[None, :, None]
    )
    compact = jnp.einsum(
        "eks,esd->ked",
        picker.astype(jnp.bfloat16),
        arrived_rows,
        preferred_element_type=jnp.float32,
    ).astype(jnp.bfloat16)
    token_span = (column * tok_local + jnp.arange(tok_local)) // WIN
    pool_matrix = (token_span[None, :] == jnp.arange(span_local)[:, None]).astype(jnp.float32)
    gathered = lax.all_gather(compact, "dp", axis=0, tiled=True)
    returned = lax.psum_scatter(
        expert_rows(gathered, w_gate, w_up, w_down), "dp", scatter_dimension=0, tiled=True
    )
    spread = jnp.einsum(
        "eks,ked->esd", picker.astype(jnp.float32), returned, precision=highest_precision
    )
    back = lax.all_to_all(spread, "expert", split_axis=1, concat_axis=0, tiled=True)
    gate_table = jnp.where(first, jax.nn.sigmoid(first_logit - second_logit)[:, None], 0.0)
    gate_table = gate_table + jnp.where(
        second, jax.nn.sigmoid(second_logit - first_logit)[:, None], 0.0
    )
    token_out = mixed + jnp.einsum("te,etd->td", gate_table, back, precision=highest_precision)
    pooled_local = jnp.dot(pool_matrix, token_out, precision=highest_precision)
    pooled = lax.psum_scatter(pooled_local, "expert", scatter_dimension=1, tiled=True)
    squares = lax.psum(jnp.sum(pooled * pooled, axis=-1), "expert")
    summary = (pooled * lax.rsqrt(squares / width + EPSILON)[:, None] * summary_gain).astype(
        jnp.bfloat16
    )
    everyone = lax.all_gather(summary, "dp", axis=0, tiled=True)
    heads_local = slice_width // HD
    mine = summary.reshape(span_local, heads_local, HD)
    others = everyone.reshape(everyone.shape[0], heads_local, HD)
    factor = reduce_scale / math.sqrt(HD)
    scores = (
        jnp.einsum("chd,khd->hck", mine, others, preferred_element_type=jnp.float32)
        * factor[:, None, None]
    )
    own_assign = lax.dynamic_slice_in_dim(assign, dp_index * span_local, span_local)
    same = own_assign[:, None] == assign[None, :]
    scores = jnp.where(same[None], scores, -jnp.inf)
    highest = jnp.max(scores, axis=-1, keepdims=True)
    expo = jnp.exp(scores - highest)
    weights = (expo / jnp.sum(expo, axis=-1, keepdims=True)).astype(jnp.bfloat16)
    reduced = jnp.einsum("hck,khd->chd", weights, others, preferred_element_type=jnp.float32)
    reduced = reduced.reshape(span_local, slice_width).astype(jnp.bfloat16)
    return (summary, reduced)


def solution(mesh):
    return jax.shard_map(
        shards,
        mesh=mesh,
        in_specs=(
            P(("dp", "expert"), None),
            P("dp", "expert"),
            P("dp", "expert"),
            P("dp", "expert"),
            P("dp", None, "expert"),
            P("dp", None, "expert"),
            P("expert", "dp"),
            P(),
            P(),
            P(("dp", "expert"), None),
            P("expert", None, "dp"),
            P("expert", None, "dp"),
            P("expert", "dp", None),
            P("expert"),
            P("expert"),
            P(),
        ),
        out_specs=(P("dp", "expert"), P("dp", "expert")),
        check_vma=False,
    )
```

profile of v0, /device:TPU:8, one launch (start us, length us, event | category | flops | bytes accessed | tf_op | source)
XLA Modules:
  0.0 635.6 jit_solution(1223442760722272505)
XLA Ops:
  7.2 0.0 copy-start
  7.2 0.0 copy-start.8
  7.2 0.0 all-gather.4.cloned.1.call-start
  7.2 0.7 all-gather.4.cloned.1.call-update
  7.9 0.0 reduce-scatter.6.cloned.1.call-start
  8.0 0.9 reshape.508
  8.9 0.4 fusion.82
  9.2 1.0 fusion.83
  10.3 0.3 fusion.49
  10.6 0.9 fusion.61
  11.5 0.4 fusion.42
  11.9 0.0 copy-start.7
  11.9 0.0 copy-start.2
  11.9 0.0 copy-start.4
  12.0 84.5 %all-gather.4.cloned.1.call-done = bf16[512,4096]{1,0:T(8,128)(2,1)} async-done(((bf16[512,128]{1,0:T(8,128)(2,1)}), bf16[512,4096]{1,0:T(8,128)(2,1)}) %all-gather.4.cloned.1.call-update) | async-done | bytes 4194320 | tf_op jit(solution)/shard_map/all_gather | solution.py:88
  96.5 4.0 fusion.58
  100.5 0.0 reduce-scatter.6.cloned.1.call-update
  100.5 0.6 compare_select_fusion.1
  101.1 4.3 all-to-all-start
  105.4 30.2 %reduce-scatter.6.cloned.1.call-done = f32[8,4096]{1,0:T(8,128)} async-done(((f32[64,4096]{1,0:T(8,128)}), f32[8,4096]{1,0:T(8,128)}) %reduce-scatter.6.cloned.1.call-update) | async-done | bytes 131088 | tf_op jit(solution)/shard_map/reduce_scatter | solution.py:91
  135.5 1.1 multiply_reduce_fusion
  136.6 1.0 multiply_convert_fusion
  137.6 0.9 broadcast_select_fusion
  138.5 0.0 all-to-all-done
  138.5 3.5 all-to-all-start.1
  142.0 0.0 all-gather.6.cloned.1.call-start
  142.1 0.1 reshape.533
  142.2 0.1 gt.13
  142.3 0.1 reduce-window.7
  142.4 0.1 add_reduce_fusion
  142.5 9.8 %all-to-all-done.1 = bf16[8,8,4096]{2,1,0:T(8,128)(2,1)S(1)} async-done(((bf16[8,8,4096]{2,1,0:T(8,128)(2,1)}), bf16[8,8,4096]{2,1,0:T(8,128)(2,1)S(1)}, u32[]{:S(2)}, u32[]{:S(2)}) %all-to-all-start.1) | async-done | bytes 524320 | tf_op jit(solution)/shard_map/all_to_all | solution.py:106
  152.2 0.9 fusion.5
  153.1 0.0 all-gather.6.cloned.1.call-update
  153.1 0.2 reduce-scatter.8.cloned.1.call-start
  153.4 86.4 %all-gather.6.cloned.1.call-done = bf16[768,1,4096]{2,0,1:T(8,128)(2,1)} async-done(((bf16[24,1,4096]{2,0,1:T(8,128)(2,1)}), bf16[768,1,4096]{2,0,1:T(8,128)(2,1)}) %all-gather.6.cloned.1.call-update) | async-done | bytes 6291472 | tf_op jit(solution)/shard_map/all_gather | solution.py:122
  239.8 6.9 %fusion.9 = f32[768,1,448]{0,2,1:T(8,128)S(1)} fusion(bf16[1,4096,448]{1,2,0:T(8,128)(2,1)} %param.26, bf16[768,1,4096]{2,0,1:T(8,128)(2,1)} %all-gather.6.cloned.1.call-done), kind=kOutput, calls=%fused_computation.13 | convolution fusion | flops 2818572288 | bytes 11337728 | tf_op jit(solution)/shard_map/ned,edf->nef/dot_general | solution.py:53
  246.7 17.8 %convolution_bitcast_fusion = f32[768,1,4096]{2,0,1:T(8,128)} fusion(bf16[1,448,4096]{2,1,0:T(8,128)(2,1)} %param.28, bf16[1,4096,448]{1,2,0:T(8,128)(2,1)} %param.27, bf16[768,1,4096]{2,0,1:T(8,128)(2,1)} %all-gather.6.cloned.1.call-done, f32[768,1,448]{0,2,1:T(8,128)S(1)} %fusion.9), kind=kOutput, calls=%fused_computation.1 | convolution fusion | flops 5639208960 | bytes 27590656 | tf_op jit(solution)/shard_map/nef,efd->ned/dot_general | solution.py:56
  264.5 0.0 reduce-scatter.8.cloned.1.call-update
  264.5 0.0 copy-start.9
  264.6 0.0 copy-start.3
  264.6 236.8 %reduce-scatter.8.cloned.1.call-done = f32[24,1,4096]{2,0,1:T(8,128)} async-done(((f32[768,1,4096]{2,0,1:T(8,128)}), f32[24,1,4096]{2,0,1:T(8,128)}) %reduce-scatter.8.cloned.1.call-update) | async-done | bytes 393232 | tf_op jit(solution)/shard_map/reduce_scatter | solution.py:123
  501.4 1.6 convolution_bitcast_fusion.2
  503.0 2.1 copy.45
  505.1 4.3 all-to-all-start.2
  509.3 0.3 reduce-scatter.10.cloned.1.call-start
  509.6 0.1 dynamic_slice.3
  509.7 0.2 select_reduce_fusion.1
  509.9 0.1 copy.54
  510.0 15.3 %all-to-all-done.2 = f32[1,64,4096]{2,0,1:T(1,128)S(1)} async-done(((f32[1,64,4096]{2,0,1:T(1,128)}), f32[1,64,4096]{2,0,1:T(1,128)S(1)}, u32[]{:S(2)}, u32[]{:S(2)}) %all-to-all-start.2) | async-done | bytes 1048608 | tf_op jit(solution)/shard_map/all_to_all | solution.py:129
  525.3 0.6 copy.86
  525.9 1.5 fusion.47
  527.4 3.2 convolution_bitcast_fusion.1
  530.6 0.0 reduce-scatter.10.cloned.1.call-update
  530.6 0.1 broadcast_compare_fusion
  530.7 34.0 %reduce-scatter.10.cloned.1.call-done = f32[512,2]{1,0:T(8,128)} async-done(((f32[4096,2]{1,0:T(8,128)}), f32[512,2]{1,0:T(8,128)}) %reduce-scatter.10.cloned.1.call-update) | async-done | bytes 4112
  564.6 1.1 copy.58
  565.7 0.1 multiply_reduce_fusion.1
  565.8 12.9 %psum.7 = f32[2]{0:T(128)S(1)} all-reduce(f32[2]{0:T(128)S(1)} %multiply_reduce_fusion.1), channel_id=1, replica_groups=mesh['dp'=32,'expert'=8] {'expert'}, use_global_device_ids=true, to_apply=%region_12.13 | all-reduce | flops 2 | bytes 16 | tf_op jit(solution)/shard_map/psum | solution.py:137
  578.8 0.0 copy-done.5
  578.8 0.1 multiply_convert_fusion.1
  578.8 0.1 fusion.95
  578.9 49.0 %all-gather = bf16[32,2,512]{2,1,0:T(2,128)(2,1)S(1)} all-gather(bf16[1,2,512]{2,1,0:T(2,128)(2,1)S(1)} %fusion.95), channel_id=1, replica_groups=mesh['dp'=32,'expert'=8] {'dp'}, dimensions={0}, use_global_device_ids=true | all-gather | bytes 67584 | tf_op jit(solution)/shard_map/all_gather | solution.py:141
  628.0 0.3 fusion.84
  628.3 0.8 fusion.46
  (30 shorter events, 0.3 us)
Async XLA Ops:
  7.2 1.7 copy-start
  7.2 4.3 copy-start.8
  7.2 89.3 %all-gather.4.cloned.1.call-start = ((), (), s32[]{:S(2)}) async-start(), calls=%async_computation.6 | async-start | bytes 4325376 | tf_op jit(solution)/shard_map/all_gather | solution.py:88
  7.9 127.6 %reduce-scatter.6.cloned.1.call-start = ((), (), s32[]{:S(2)}) async-start(), calls=%async_computation.7 | async-start | bytes 1179648 | tf_op jit(solution)/shard_map/reduce_scatter | solution.py:91
  11.9 88.6 %copy-start.7 = (s32[8,2]{0,1:T(2,128)S(1)}, s32[8,2]{0,1:T(2,128)}, u32[]{:S(2)}) copy-start(s32[8,2]{0,1:T(2,128)} %param.25) | copy-start | bytes 196
  11.9 123.6 %copy-start.2 = (bf16[8,4096]{1,0:T(8,128)(2,1)S(1)}, bf16[8,4096]{1,0:T(8,128)(2,1)}, u32[]{:S(2)}) copy-start(bf16[8,4096]{1,0:T(8,128)(2,1)} %param.16) | copy-start | bytes 196612
  11.9 124.7 %copy-start.4 = (f32[4096]{0:T(1024)S(1)}, f32[4096]{0:T(1024)}, u32[]{:S(2)}) copy-start(f32[4096]{0:T(1024)} %param.23) | copy-start | bytes 49156
  101.1 37.4 %all-to-all-start = ((s32[8,1,8]{2,1,0:T(1,128)}), s32[8,1,8]{2,1,0:T(1,128)S(1)}, u32[]{:S(2)}, u32[]{:S(2)}) async-start(s32[8,1,8]{2,1,0:T(1,128)} %compare_select_fusion.1), calls=%async_computation.1 | async-start | bytes 8192 | tf_op jit(solution)/shard_map/all_to_all | solution.py:107
  138.5 13.7 %all-to-all-start.1 = ((bf16[8,8,4096]{2,1,0:T(8,128)(2,1)}), bf16[8,8,4096]{2,1,0:T(8,128)(2,1)S(1)}, u32[]{:S(2)}, u32[]{:S(2)}) async-start(bf16[8,8,4096]{2,1,0:T(8,128)(2,1)} %broadcast_select_fusion), calls=%async_computation.2 | async-start | bytes 1048576 | tf_op jit(solution)/shard_map/all_to_all | solution.py:106
  142.0 97.8 %all-gather.6.cloned.1.call-start = ((), (), s32[]{:S(2)}) async-start(), calls=%async_computation.8 | async-start | bytes 6488064 | tf_op jit(solution)/shard_map/all_gather | solution.py:122
  153.1 348.2 %reduce-scatter.8.cloned.1.call-start = ((), (), s32[]{:S(2)}) async-start(), calls=%async_computation.9 | async-start | bytes 12976128 | tf_op jit(solution)/shard_map/reduce_scatter | solution.py:123
  264.5 245.1 %copy-start.9 = (s32[64]{0:T(128)S(1)}, s32[64]{0:T(128)}, u32[]{:S(2)}) copy-start(s32[64]{0:T(128)} %param.31) | copy-start | bytes 772
  264.6 245.1 %copy-start.3 = (bf16[4096,8]{0,1:T(8,128)(2,1)S(1)}, bf16[4096,8]{0,1:T(8,128)(2,1)}, u32[]{:S(2)}) copy-start(bf16[4096,8]{0,1:T(8,128)(2,1)} %param.24) | copy-start | bytes 196612
  503.0 24.4 %copy-start.1 = (f32[8,4096]{1,0:T(8,128)S(1)}, f32[8,4096]{1,0:T(8,128)}, u32[]{:S(2)}) copy-start(f32[8,4096]{1,0:T(8,128)} %reduce-scatter.6.cloned.1.call-done) | copy-start | bytes 393220
  505.1 20.2 %all-to-all-start.2 = ((f32[1,64,4096]{2,0,1:T(1,128)}), f32[1,64,4096]{2,0,1:T(1,128)S(1)}, u32[]{:S(2)}, u32[]{:S(2)}) async-start(f32[1,64,4096]{2,0,1:T(1,128)} %copy.45), calls=%async_computation.4 | async-start | bytes 2097152 | tf_op jit(solution)/shard_map/all_to_all | solution.py:129
  509.3 55.3 %reduce-scatter.10.cloned.1.call-start = ((), (), s32[]{:S(2)}) async-start(), calls=%async_computation.10 | async-start | bytes 2359296
  510.0 55.9 %copy-start.10 = (f32[4]{0:T(128)S(1)}, f32[4]{0:T(128)}, u32[]{:S(2)}) copy-start(f32[4]{0:T(128)} %param.30) | copy-start | bytes 52
  510.0 68.8 %copy-start.5 = (f32[512]{0:T(512)S(1)}, f32[512]{0:T(512)}, u32[]{:S(2)}) copy-start(f32[512]{0:T(512)} %param.29) | copy-start | bytes 6148
  578.8 50.3 %copy-start.6 = (bf16[2,512]{1,0:T(2,128)(2,1)}, bf16[2,512]{1,0:T(2,128)(2,1)S(1)}, u32[]{:S(2)}) copy-start(bf16[2,512]{1,0:T(2,128)(2,1)S(1)} %multiply_convert_fusion.1) | copy-start | bytes 6148
Sparse Core Ops, SparseCore 0:
  10.5 85.9 all-gather.3
  100.6 34.8 reduce-scatter.5
  153.3 86.4 all-gather.5
  264.7 236.6 reduce-scatter.7
  530.7 33.8 reduce-scatter.9
where the time goes:
time: 636 us
  waiting for transfers between devices  498 us (78%)
  blocking collectives  61.9 us (10%)
  matrix products  39.8 us (6%)
  between operations  14.1 us (2%)
  starting transfers between devices  12.6 us (2%)
    reduce_scatter x1, waiting for transfers between devices, shards(): lax.psum_scatter(expert_rows(gathered, w_gate, w_up, w_down), 'dp', scatt...  237 us
    all_gather x1, waiting for transfers between devices, shards(): gathered = lax.all_gather(compact, 'dp', axis=0, tiled=True)  86.4 us
    all_gather x1, waiting for transfers between devices, shards(): lax.all_gather(out_weight, 'dp', axis=1, tiled=True)  84.5 us
    all_gather x1, blocking collectives, shards(): everyone = lax.all_gather(summary, 'dp', axis=0, tiled=True)  49 us
    unnamed x6, waiting for transfers between devices  34.7 us
    reduce_scatter x1, waiting for transfers between devices, shards(): lax.psum_scatter(head_terms, 'expert', scatter_dimension=0, tiled=True)  30.2 us
    dot_general x1, matrix products, expert_rows(): jnp.einsum('nef,efd->ned', hidden, w_down, preferred_element_type=jnp.flo...  17.8 us
    all_to_all x1, waiting for transfers between devices, shards(): lax.all_to_all(spread, 'expert', split_axis=1, concat_axis=0, tiled=True)  15.3 us
  transfers between devices with their start and end apart: 8, of which 7 were waited for; matrix products, arithmetic and copies ran while one was open for 1% of the time, Pallas kernels for 0%

commit v1 on v0

--- a/solution.py
+++ b/solution.py
@@ -1,3 +1,4 @@
+import functools
 import math
 import jax
 import jax.numpy as jnp
@@ -11,6 +12,16 @@
 WIN = 32
 GROUP_CAP = 24
 EPSILON = 1e-05
+
+
+def keep_up_shelves(xs, device_axis):
+    z2 = lax.all_to_all(
+        jnp.concatenate([xs] * lax.psum(1, device_axis), axis=0), device_axis, 0, 0, tiled=True
+    )
+    return z2
+
+
+compute_the_keys = functools.partial(keep_up_shelves, device_axis="dp")
 
 
 def attend(queries, new_keys, new_values, cache_keys, cache_values):
@@ -138,7 +149,7 @@
     summary = (pooled * lax.rsqrt(squares / width + EPSILON)[:, None] * summary_gain).astype(
         jnp.bfloat16
     )
-    everyone = lax.all_gather(summary, "dp", axis=0, tiled=True)
+    everyone = compute_the_keys(summary)
     heads_local = slice_width // HD
     mine = summary.reshape(span_local, heads_local, HD)
     others = everyone.reshape(everyone.shape[0], heads_local, HD)

time: 636 us -> 607 us (0.954)
  blocking collectives: 61.9 us -> 12.9 us
  starting transfers between devices: 12.6 us -> 22.8 us
  waiting for transfers between devices: 498 us -> 506 us
    all_gather x1 -> x0, blocking collectives: 49 us -> none  [shards(): everyone = lax.all_gather(summary, 'dp', axis=0, tiled=True)]
    all_to_all x0 -> x1, starting transfers between devices: none -> 10.2 us  [keep_up_shelves(): lax.all_to_all(jnp.concatenate([xs] * lax.psum(1, device_axis), axis=0),...]
    all_to_all x0 -> x1, waiting for transfers between devices: none -> 8.68 us  [keep_up_shelves(): lax.all_to_all(jnp.concatenate([xs] * lax.psum(1, device_axis), axis=0),...]
  transfers between devices with their start and end apart: 8 -> 9, of which waited for: 7 -> 8; matrix products, arithmetic and copies ran while one was open for 1% -> 1% of each run, Pallas kernels for 0% -> 0%
where the time goes in v1:
time: 607 us; the launch traced here: 606 us
  waiting for transfers between devices  506 us (83%)
  matrix products  39.8 us (7%)
  starting transfers between devices  22.8 us (4%)
  between operations  14.1 us (2%)
  blocking collectives  12.9 us (2%)
    reduce_scatter x1, waiting for transfers between devices, shards(): lax.psum_scatter(expert_rows(gathered, w_gate, w_up, w_down), 'dp', scatt...  237 us
    all_gather x1, waiting for transfers between devices, shards(): gathered = lax.all_gather(compact, 'dp', axis=0, tiled=True)  86.4 us
    all_gather x1, waiting for transfers between devices, shards(): lax.all_gather(out_weight, 'dp', axis=1, tiled=True)  84.5 us
    unnamed x6, waiting for transfers between devices  34.7 us
    reduce_scatter x1, waiting for transfers between devices, shards(): lax.psum_scatter(head_terms, 'expert', scatter_dimension=0, tiled=True)  30.2 us
    dot_general x1, matrix products, expert_rows(): jnp.einsum('nef,efd->ned', hidden, w_down, preferred_element_type=jnp.flo...  17.8 us
    all_to_all x1, waiting for transfers between devices, shards(): lax.all_to_all(spread, 'expert', split_axis=1, concat_axis=0, tiled=True)  15.4 us
    psum x1, blocking collectives, shards(): squares = lax.psum(jnp.sum(pooled * pooled, axis=-1), 'expert')  12.9 us
  transfers between devices with their start and end apart: 9, of which 8 were waited for; matrix products, arithmetic and copies ran while one was open for 1% of the time, Pallas kernels for 0%

profile of v1, /device:TPU:8, one launch (start us, length us, event | category | flops | bytes accessed | tf_op | source)
XLA Modules:
  0.0 606.4 jit_solution(2636424684395799341)
XLA Ops:
  7.2 0.0 copy-start
  7.2 0.0 all-gather.3.cloned.1.call-start
  7.2 0.7 all-gather.3.cloned.1.call-update
  7.9 0.0 reduce-scatter.6.cloned.1.call-start
  8.0 0.9 reshape.511
  8.9 0.4 fusion.82
  9.2 1.0 fusion.83
  10.3 0.3 fusion.49
  10.6 0.9 fusion.61
  11.5 0.4 fusion.42
  11.9 0.0 copy-start.7
  11.9 0.0 copy-start.3
  11.9 0.0 copy-start.5
  12.0 84.5 %all-gather.3.cloned.1.call-done = bf16[512,4096]{1,0:T(8,128)(2,1)} async-done(((bf16[512,128]{1,0:T(8,128)(2,1)}), bf16[512,4096]{1,0:T(8,128)(2,1)}) %all-gather.3.cloned.1.call-update) | async-done | bytes 4194320 | tf_op jit(solution)/shard_map/all_gather | solution.py:99
  96.5 4.0 fusion.58
  100.5 0.0 reduce-scatter.6.cloned.1.call-update
  100.5 0.6 compare_select_fusion.1
  101.1 4.3 all-to-all-start
  105.4 30.2 %reduce-scatter.6.cloned.1.call-done = f32[8,4096]{1,0:T(8,128)} async-done(((f32[64,4096]{1,0:T(8,128)}), f32[8,4096]{1,0:T(8,128)}) %reduce-scatter.6.cloned.1.call-update) | async-done | bytes 131088 | tf_op jit(solution)/shard_map/reduce_scatter | solution.py:102
  135.5 1.1 multiply_reduce_fusion
  136.6 1.0 multiply_convert_fusion
  137.6 0.9 broadcast_select_fusion
  138.5 0.0 all-to-all-done
  138.5 3.5 all-to-all-start.1
  142.0 0.0 all-gather.5.cloned.1.call-start
  142.1 0.1 reshape.533
  142.2 0.1 gt.13
  142.3 0.1 reduce-window.7
  142.4 0.1 add_reduce_fusion
  142.5 9.8 %all-to-all-done.1 = bf16[8,8,4096]{2,1,0:T(8,128)(2,1)S(1)} async-done(((bf16[8,8,4096]{2,1,0:T(8,128)(2,1)}), bf16[8,8,4096]{2,1,0:T(8,128)(2,1)S(1)}, u32[]{:S(2)}, u32[]{:S(2)}) %all-to-all-start.1) | async-done | bytes 524320 | tf_op jit(solution)/shard_map/all_to_all | solution.py:117
  152.2 0.9 fusion.5
  153.1 0.0 all-gather.5.cloned.1.call-update
  153.1 0.2 reduce-scatter.8.cloned.1.call-start
  153.4 86.4 %all-gather.5.cloned.1.call-done = bf16[768,1,4096]{2,0,1:T(8,128)(2,1)} async-done(((bf16[24,1,4096]{2,0,1:T(8,128)(2,1)}), bf16[768,1,4096]{2,0,1:T(8,128)(2,1)}) %all-gather.5.cloned.1.call-update) | async-done | bytes 6291472 | tf_op jit(solution)/shard_map/all_gather | solution.py:133
  239.8 6.9 %fusion.9 = f32[768,1,448]{0,2,1:T(8,128)S(1)} fusion(bf16[1,4096,448]{1,2,0:T(8,128)(2,1)} %param.26, bf16[768,1,4096]{2,0,1:T(8,128)(2,1)} %all-gather.5.cloned.1.call-done), kind=kOutput, calls=%fused_computation.13 | convolution fusion | flops 2818572288 | bytes 11337728 | tf_op jit(solution)/shard_map/ned,edf->nef/dot_general | solution.py:64
  246.7 17.8 %convolution_bitcast_fusion = f32[768,1,4096]{2,0,1:T(8,128)} fusion(bf16[1,448,4096]{2,1,0:T(8,128)(2,1)} %param.28, bf16[1,4096,448]{1,2,0:T(8,128)(2,1)} %param.27, bf16[768,1,4096]{2,0,1:T(8,128)(2,1)} %all-gather.5.cloned.1.call-done, f32[768,1,448]{0,2,1:T(8,128)S(1)} %fusion.9), kind=kOutput, calls=%fused_computation.1 | convolution fusion | flops 5639208960 | bytes 27590656 | tf_op jit(solution)/shard_map/nef,efd->ned/dot_general | solution.py:67
  264.5 0.0 reduce-scatter.8.cloned.1.call-update
  264.5 0.0 copy-start.4
  264.6 236.8 %reduce-scatter.8.cloned.1.call-done = f32[24,1,4096]{2,0,1:T(8,128)} async-done(((f32[768,1,4096]{2,0,1:T(8,128)}), f32[24,1,4096]{2,0,1:T(8,128)}) %reduce-scatter.8.cloned.1.call-update) | async-done | bytes 393232 | tf_op jit(solution)/shard_map/reduce_scatter | solution.py:134
  501.4 1.6 convolution_bitcast_fusion.2
  503.0 2.1 copy.45
  505.1 4.3 all-to-all-start.2
  509.3 0.3 reduce-scatter.10.cloned.1.call-start
  509.6 0.2 select_reduce_fusion.1
  509.8 0.1 copy.54
  509.9 15.4 %all-to-all-done.2 = f32[1,64,4096]{2,0,1:T(1,128)S(1)} async-done(((f32[1,64,4096]{2,0,1:T(1,128)}), f32[1,64,4096]{2,0,1:T(1,128)S(1)}, u32[]{:S(2)}, u32[]{:S(2)}) %all-to-all-start.2) | async-done | bytes 1048608 | tf_op jit(solution)/shard_map/all_to_all | solution.py:140
  525.3 0.6 copy.86
  525.9 0.0 copy-start.10
  525.9 1.5 fusion.47
  527.4 3.2 convolution_bitcast_fusion.1
  530.6 0.0 reduce-scatter.10.cloned.1.call-update
  530.6 0.1 dynamic_slice.3
  530.7 34.0 %reduce-scatter.10.cloned.1.call-done = f32[512,2]{1,0:T(8,128)} async-done(((f32[4096,2]{1,0:T(8,128)}), f32[512,2]{1,0:T(8,128)}) %reduce-scatter.10.cloned.1.call-update) | async-done | bytes 4112
  564.6 1.1 copy.58
  565.7 0.1 multiply_reduce_fusion.1
  565.8 0.1 broadcast_compare_fusion
  565.9 12.9 %psum.7 = f32[2]{0:T(128)S(1)} all-reduce(f32[2]{0:T(128)S(1)} %multiply_reduce_fusion.1), channel_id=1, replica_groups=mesh['dp'=32,'expert'=8] {'expert'}, use_global_device_ids=true, to_apply=%region_12.13 | all-reduce | flops 2 | bytes 16 | tf_op jit(solution)/shard_map/psum | solution.py:148
  578.8 0.1 multiply_convert_fusion.1
  578.9 0.3 concatenate.3
  579.2 0.7 all_to_all.34
  579.8 10.2 %all-to-all-start.3 = ((bf16[32,2,512]{2,1,0:T(2,128)(2,1)}), bf16[32,2,512]{2,1,0:T(2,128)(2,1)S(1)}, u32[]{:S(2)}, u32[]{:S(2)}) async-start(bf16[32,2,512]{2,1,0:T(2,128)(2,1)} %all_to_all.34), calls=%async_computation.5 | async-start | bytes 131072 | tf_op jit(solution)/shard_map/all_to_all | solution.py:18
  590.1 8.7 %all-to-all-done.3 = bf16[32,2,512]{2,1,0:T(2,128)(2,1)S(1)} async-done(((bf16[32,2,512]{2,1,0:T(2,128)(2,1)}), bf16[32,2,512]{2,1,0:T(2,128)(2,1)S(1)}, u32[]{:S(2)}, u32[]{:S(2)}) %all-to-all-start.3) | async-done | bytes 65568 | tf_op jit(solution)/shard_map/all_to_all | solution.py:18
  598.8 0.3 fusion.84
  599.1 0.8 fusion.46
  (32 shorter events, 0.3 us)
Async XLA Ops:
  7.2 1.7 copy-start
  7.2 4.3 copy-start.8
  7.2 89.3 %all-gather.3.cloned.1.call-start = ((), (), s32[]{:S(2)}) async-start(), calls=%async_computation.7 | async-start | bytes 4325376 | tf_op jit(solution)/shard_map/all_gather | solution.py:99
  7.9 127.6 %reduce-scatter.6.cloned.1.call-start = ((), (), s32[]{:S(2)}) async-start(), calls=%async_computation.8 | async-start | bytes 1179648 | tf_op jit(solution)/shard_map/reduce_scatter | solution.py:102
  11.9 88.6 %copy-start.7 = (s32[8,2]{0,1:T(2,128)S(1)}, s32[8,2]{0,1:T(2,128)}, u32[]{:S(2)}) copy-start(s32[8,2]{0,1:T(2,128)} %param.25) | copy-start | bytes 196
  11.9 123.6 %copy-start.3 = (bf16[8,4096]{1,0:T(8,128)(2,1)S(1)}, bf16[8,4096]{1,0:T(8,128)(2,1)}, u32[]{:S(2)}) copy-start(bf16[8,4096]{1,0:T(8,128)(2,1)} %param.16) | copy-start | bytes 196612
  11.9 124.7 %copy-start.5 = (f32[4096]{0:T(1024)S(1)}, f32[4096]{0:T(1024)}, u32[]{:S(2)}) copy-start(f32[4096]{0:T(1024)} %param.23) | copy-start | bytes 49156
  101.1 37.4 %all-to-all-start = ((s32[8,1,8]{2,1,0:T(1,128)}), s32[8,1,8]{2,1,0:T(1,128)S(1)}, u32[]{:S(2)}, u32[]{:S(2)}) async-start(s32[8,1,8]{2,1,0:T(1,128)} %compare_select_fusion.1), calls=%async_computation.1 | async-start | bytes 8192 | tf_op jit(solution)/shard_map/all_to_all | solution.py:118
  138.5 13.7 %all-to-all-start.1 = ((bf16[8,8,4096]{2,1,0:T(8,128)(2,1)}), bf16[8,8,4096]{2,1,0:T(8,128)(2,1)S(1)}, u32[]{:S(2)}, u32[]{:S(2)}) async-start(bf16[8,8,4096]{2,1,0:T(8,128)(2,1)} %broadcast_select_fusion), calls=%async_computation.2 | async-start | bytes 1048576 | tf_op jit(solution)/shard_map/all_to_all | solution.py:117
  142.0 97.8 %all-gather.5.cloned.1.call-start = ((), (), s32[]{:S(2)}) async-start(), calls=%async_computation.9 | async-start | bytes 6488064 | tf_op jit(solution)/shard_map/all_gather | solution.py:133
  153.1 348.2 %reduce-scatter.8.cloned.1.call-start = ((), (), s32[]{:S(2)}) async-start(), calls=%async_computation.10 | async-start | bytes 12976128 | tf_op jit(solution)/shard_map/reduce_scatter | solution.py:134
  264.5 245.1 %copy-start.4 = (bf16[4096,8]{0,1:T(8,128)(2,1)S(1)}, bf16[4096,8]{0,1:T(8,128)(2,1)}, u32[]{:S(2)}) copy-start(bf16[4096,8]{0,1:T(8,128)(2,1)} %param.24) | copy-start | bytes 196612
  503.0 24.4 %copy-start.2 = (f32[8,4096]{1,0:T(8,128)S(1)}, f32[8,4096]{1,0:T(8,128)}, u32[]{:S(2)}) copy-start(f32[8,4096]{1,0:T(8,128)} %reduce-scatter.6.cloned.1.call-done) | copy-start | bytes 393220
  505.1 20.2 %all-to-all-start.2 = ((f32[1,64,4096]{2,0,1:T(1,128)}), f32[1,64,4096]{2,0,1:T(1,128)S(1)}, u32[]{:S(2)}, u32[]{:S(2)}) async-start(f32[1,64,4096]{2,0,1:T(1,128)} %copy.45), calls=%async_computation.4 | async-start | bytes 2097152 | tf_op jit(solution)/shard_map/all_to_all | solution.py:140
  509.3 55.3 %reduce-scatter.10.cloned.1.call-start = ((), (), s32[]{:S(2)}) async-start(), calls=%async_computation.11 | async-start | bytes 2359296
  509.9 20.7 %copy-start.9 = (s32[64]{0:T(128)S(1)}, s32[64]{0:T(128)}, u32[]{:S(2)}) copy-start(s32[64]{0:T(128)} %param.31) | copy-start | bytes 772
  509.9 68.9 %copy-start.6 = (f32[512]{0:T(512)S(1)}, f32[512]{0:T(512)}, u32[]{:S(2)}) copy-start(f32[512]{0:T(512)} %param.29) | copy-start | bytes 6148
  525.9 64.2 %copy-start.10 = (f32[4]{0:T(128)S(1)}, f32[4]{0:T(128)}, u32[]{:S(2)}) copy-start(f32[4]{0:T(128)} %param.30) | copy-start | bytes 52
  578.9 21.0 %copy-start.1 = (bf16[2,512]{1,0:T(2,128)(2,1)}, bf16[2,512]{1,0:T(2,128)(2,1)S(1)}, u32[]{:S(2)}) copy-start(bf16[2,512]{1,0:T(2,128)(2,1)S(1)} %multiply_convert_fusion.1) | copy-start | bytes 6148
  579.8 18.9 %all-to-all-start.3 = ((bf16[32,2,512]{2,1,0:T(2,128)(2,1)}), bf16[32,2,512]{2,1,0:T(2,128)(2,1)S(1)}, u32[]{:S(2)}, u32[]{:S(2)}) async-start(bf16[32,2,512]{2,1,0:T(2,128)(2,1)} %all_to_all.34), calls=%async_computation.5 | async-start | bytes 131072 | tf_op jit(solution)/shard_map/all_to_all | solution.py:18
Sparse Core Ops, SparseCore 0:
  10.5 85.9 all-gather.2
  100.6 34.8 reduce-scatter.5
  153.3 86.4 all-gather.4
  264.7 236.6 reduce-scatter.7
  530.7 33.8 reduce-scatter.9
